TPU v7x, 32 devices: a whole 2x2x4 slice. The times are simulated.
32 devices in a mesh: lon: 8 (over y, x, core), lat: 4 (over z).
Axes of the slice: x: 2, y: 2, z: 4, core: 2. Of those that a mesh axis runs over, the one named last changes fastest.
Arguments:
- obs_rows: bfloat16 [131072, 128], P(('lon', 'lat')), may hold values from -6 to 6
- cell_ids: int32 [131072], P(('lon', 'lat')), may hold values from 0 to 511
- counts: int32 [32, 32], P(('lon', 'lat')), may hold values from 16 to 128, as said below
- w_embed: bfloat16 [128, 256], replicated, may hold values from -0.5 to 0.5
- w_density: bfloat16 [256], replicated, may hold values from -3 to 3
- kernels: bfloat16 [3, 3, 3, 256, 256], replicated, may hold values from -0.125 to 0.125
- cotangent: bfloat16 [64, 256, 256], P('lat', 'lon'), may hold values from -6 to 6
Outputs:
- encoded: bfloat16 [64, 256, 256], P('lat', 'lon')
- grad_kernels: bfloat16 [3, 3, 3, 256, 256], replicated
- grad_embed: bfloat16 [128, 256], replicated
- grad_obs: bfloat16 [131072, 128], P(('lon', 'lat'))
Inputs may be any that keep to these rules, and one draw needn't show every extreme that they name: `counts`: the live rows of each slot are its first ones; in every draw some tile owner receives 128 live rows from every device.
All inputs are finite; a program needn't handle non-finite values.
Results may differ from a plain program's by a relative error of at most 0.011.
Values may be sent and summed in bfloat16 or wider, within the bound.
No kernel may reach another device: no remote copies, remote signals or barrier semaphores. Data moves between devices by JAX's collectives and lax.ppermute only.
A program may use at most 128 MiB of HBM per device.

v0:
```python
import math
import jax
import jax.numpy as jnp
from jax import lax
from jax.sharding import PartitionSpec as P


def extended(block, sides, width, periodic):
    for axis, dim in sides:
        count = lax.axis_size(axis)
        forward = [(i, i + 1) for i in range(count - 1)]
        if periodic:
            forward.append((count - 1, 0))
        backward = [(target, source) for source, target in forward]
        low = lax.ppermute(
            lax.slice_in_dim(block, block.shape[dim] - width, None, axis=dim), axis, forward
        )
        high = lax.ppermute(lax.slice_in_dim(block, 0, width, axis=dim), axis, backward)
        block = jnp.concatenate([low, block, high], axis=dim)
    return block


def add_rims(field):
    widened = extended(field, (("lon", 1),), 1, True)
    return extended(widened, (("lat", 0),), 1, False)


def conv_valid(padded, kernel):
    return lax.conv_general_dilated(
        padded[None],
        kernel,
        (1, 1),
        "VALID",
        dimension_numbers=("NHWC", "HWIO", "NHWC"),
        preferred_element_type=jnp.float32,
    )[0]


def on_device(obs_rows, cell_ids, counts, w_embed, w_density, kernels, cotangent):
    lon_count = lax.axis_size("lon")
    lat_count = lax.axis_size("lat")
    devices = lon_count * lat_count
    height, tile_width, channels = cotangent.shape
    cell_count = height * tile_width
    slot_rows = obs_rows.shape[0] // devices
    feat_count = obs_rows.shape[1]
    layer_count = kernels.shape[0]
    live_mask = (jnp.arange(slot_rows, dtype=jnp.int32)[None, :] < counts[0][:, None]).reshape(-1)
    sent_ids = jnp.where(live_mask, cell_ids, -1)
    got_rows, got_ids = (
        lax.all_to_all(obs_rows, ("lon", "lat"), split_axis=0, concat_axis=0, tiled=True),
        lax.all_to_all(sent_ids, ("lon", "lat"), split_axis=0, concat_axis=0, tiled=True),
    )
    row_total = got_rows.shape[0]
    block_rows = math.gcd(row_total, 2048)
    cell_iota = jnp.arange(cell_count, dtype=jnp.int32)

    def accumulate(turn_index, running):
        cell_sums, density = running
        begin = turn_index * block_rows
        block_ids = lax.dynamic_slice_in_dim(got_ids, begin, block_rows)
        block_feats = lax.dynamic_slice_in_dim(got_rows, begin, block_rows, 0)
        hit_mask = block_ids[:, None] == cell_iota[None, :]
        onehot = hit_mask.astype(jnp.bfloat16)
        cell_sums = cell_sums + lax.dot_general(
            onehot, block_feats, (((0,), (0,)), ((), ())), preferred_element_type=jnp.float32
        )
        density = density + jnp.sum(hit_mask.astype(jnp.float32), axis=0)
        return (cell_sums, density)

    cell_sums, density = lax.fori_loop(
        0,
        row_total // block_rows,
        accumulate,
        (jnp.zeros((cell_count, feat_count), jnp.float32), jnp.zeros((cell_count,), jnp.float32)),
    )
    inv_root = lax.rsqrt(density + 1.0)
    features = (cell_sums * inv_root[:, None]).astype(jnp.bfloat16)
    start_act = (
        jnp.dot(features, w_embed, preferred_element_type=jnp.float32)
        + jnp.log1p(density)[:, None] * w_density.astype(jnp.float32)[None, :]
    )
    activation = start_act.astype(jnp.bfloat16).reshape(height, tile_width, channels)
    stored_pads = []
    stored_pre = []
    for layer_index in range(layer_count):
        padded = add_rims(activation)
        preact = conv_valid(padded, kernels[layer_index])
        stored_pads.append(padded)
        stored_pre.append(preact)
        activation = (activation.astype(jnp.float32) + jax.nn.silu(preact)).astype(jnp.bfloat16)
    grad_scale = 1.0 / math.sqrt(cell_count * devices)
    back_low = cotangent
    kernel_grads = [None] * layer_count
    for layer_index in reversed(range(layer_count)):
        preact = stored_pre[layer_index]
        sigmoid_v = jax.nn.sigmoid(preact)
        slope_bf = (
            back_low.astype(jnp.float32) * (sigmoid_v * (1.0 + preact * (1.0 - sigmoid_v)))
        ).astype(jnp.bfloat16)
        slope_flat = slope_bf.reshape(cell_count, channels)
        padded = stored_pads[layer_index]
        tap_rows = []
        for row_off in range(3):
            tap_cols = []
            for col_off in range(3):
                window = padded[row_off : row_off + height, col_off : col_off + tile_width].reshape(
                    cell_count, channels
                )
                tap_cols.append(
                    lax.dot_general(
                        window,
                        slope_flat,
                        (((0,), (0,)), ((), ())),
                        preferred_element_type=jnp.float32,
                    )
                )
            tap_rows.append(jnp.stack(tap_cols))
        tap_grad = jnp.stack(tap_rows) * grad_scale
        kernel_grads[layer_index] = tap_grad
        flipped = jnp.transpose(kernels[layer_index][::-1, ::-1], (0, 1, 3, 2))
        spread = conv_valid(add_rims(slope_bf), flipped)
        back_low = lax.optimization_barrier(
            (back_low.astype(jnp.float32) + spread).astype(jnp.bfloat16)
        )
    back_flat = back_low.reshape(cell_count, channels)
    embed_grad = (
        lax.dot_general(
            features, back_flat, (((0,), (0,)), ((), ())), preferred_element_type=jnp.float32
        )
        * grad_scale
    )
    cell_grad = (
        lax.dot_general(
            back_flat, w_embed, (((1,), (1,)), ((), ())), preferred_element_type=jnp.float32
        )
        * inv_root[:, None]
    ).astype(jnp.bfloat16)
    kernel_total, embed_total = lax.psum((jnp.stack(kernel_grads), embed_grad), ("lon", "lat"))
    kernel_out = kernel_total.astype(jnp.bfloat16)
    embed_out = embed_total.astype(jnp.bfloat16)
    picked = jnp.take(cell_grad, jnp.maximum(got_ids, 0), axis=0)
    picked = jnp.where((got_ids >= 0)[:, None], picked, jnp.zeros_like(picked))
    grad_obs = lax.all_to_all(picked, ("lon", "lat"), split_axis=0, concat_axis=0, tiled=True)
    return (activation, kernel_out, embed_out, grad_obs)


def solution(mesh):
    placed = (
        P(("lon", "lat"), None),
        P(("lon", "lat")),
        P(("lon", "lat"), None),
        P(),
        P(),
        P(),
        P("lat", "lon", None),
    )
    return jax.shard_map(
        on_device,
        mesh=mesh,
        in_specs=placed,
        out_specs=(P("lat", "lon", None), P(), P(), P(("lon", "lat"), None)),
        check_vma=False,
    )
```

profile of v0, /device:TPU:0, one launch (start us, length us, event | category | flops | bytes accessed | tf_op | source)
XLA Modules:
  0.0 306.9 jit_solution(6988521680574470004)
XLA Ops:
  1.5 14.3 %all_to_all.33 = s32[32,128,1]{1,2,0:T(1,128)S(1)} all-to-all(s32[32,128,1]{1,2,0:T(1,128)S(1)} %bitcast.270), channel_id=1, replica_groups=mesh['lon'=8,'lat'=4] {'lon','lat'}, dimensions={0} | all-to-all | bytes 32768 | tf_op jit(solution)/shard_map/all_to_all | solution.py:52
  15.7 2.6 all-to-all-start.1
  19.1 24.4 %all-to-all-done.1 = bf16[32,128,128]{2,1,0:T(8,128)(2,1)S(1)} async-done(((bf16[32,128,128]{2,1,0:T(8,128)(2,1)}), bf16[32,128,128]{2,1,0:T(8,128)(2,1)S(1)}, u32[]{:S(2)}, u32[]{:S(2)}) %all-to-all-start.1) | async-done | bytes 1048608 | tf_op jit(solution)/shard_map/all_to_all | solution.py:51
  43.4 4.4 %while.16 = (s32[]{:T(128)}, f32[512,128]{1,0:T(8,128)S(1)}, f32[512]{0:T(512)S(1)}, s32[4096]{0:T(1024)S(1)}, bf16[4096,128]{1,0:T(8,128)(2,1)S(1)}, /*index=5*/s32[]{:T(128)}, s32[]{:T(128)}, s32[]{:T(128)}, s32[]{:T(128)}) while((s32[]{:T(128)}, f32[512,128]{1,0:T(8,128)S(1)}, f32[512]{0:T(512)S(1)}, s32[4096]{0:T(1024)S(1)}, ...), condition=%wide.region_2.3_spmd.clone, body=%wide.region_0.2_spmd.clone.sunk | while | flops 272761344 | bytes 1089702 | solution.py:71
  44.0 1.6 fusion.171
  46.3 1.6 fusion.171
  48.2 1.6 collective-permute-start
  51.0 1.4 collective-permute-done
  52.4 5.1 %collective-permute-start.2 = (bf16[1,34,256]{2,1,0:T(8,128)(2,1)S(1)}, bf16[1,34,256]{2,1,0:T(8,128)(2,1)S(1)}, u32[]{:S(2)}, u32[]{:S(2)}) collective-permute-start(bf16[1,34,256]{2,1,0:T(8,128)(2,1)S(1)} %get-tuple-element.166), channel_id=1, source_target_pairs={{0,1},{1,2},{2,3},{4,5},{5,6},{6,7},{8,9},{9,10},{10,11},{12,13},{... | collective-permute-start | bytes 52232 | tf_op jit(solution)/shard_map/ppermute | solution.py:15
  57.5 1.3 collective-permute-start.3
  59.0 4.2 %collective-permute-done.3 = bf16[1,34,256]{2,1,0:T(8,128)(2,1)S(1)} collective-permute-done((bf16[1,34,256]{2,1,0:T(8,128)(2,1)S(1)}, bf16[1,34,256]{2,1,0:T(8,128)(2,1)S(1)}, u32[]{:S(2)}, u32[]{:S(2)}) %collective-permute-start.3) | collective-permute-done | bytes 17440 | tf_op jit(solution)/shard_map/ppermute | solution.py:18
  65.4 2.6 collective-permute-start.5
  68.0 1.4 collective-permute-done.4
  69.5 1.9 collective-permute-start.6
  72.8 4.2 %collective-permute-done.7 = bf16[1,34,256]{2,1,0:T(8,128)(2,1)S(1)} collective-permute-done((bf16[1,34,256]{2,1,0:T(8,128)(2,1)S(1)}, bf16[1,34,256]{2,1,0:T(8,128)(2,1)S(1)}, u32[]{:S(2)}, u32[]{:S(2)}) %collective-permute-start.7) | collective-permute-done | bytes 17440 | tf_op jit(solution)/shard_map/ppermute | solution.py:18
  79.2 2.6 collective-permute-start.9
  83.3 3.0 collective-permute-start.10
  87.8 4.1 %collective-permute-done.11 = bf16[1,34,256]{2,1,0:T(8,128)(2,1)S(1)} collective-permute-done((bf16[1,34,256]{2,1,0:T(8,128)(2,1)S(1)}, bf16[1,34,256]{2,1,0:T(8,128)(2,1)S(1)}, u32[]{:S(2)}, u32[]{:S(2)}) %collective-permute-start.11) | collective-permute-done | bytes 17440 | tf_op jit(solution)/shard_map/ppermute | solution.py:18
  97.7 2.6 collective-permute-start.13
  101.8 1.9 collective-permute-start.14
  105.3 4.1 %collective-permute-done.15 = bf16[1,34,256]{2,1,0:T(8,128)(2,1)S(1)} collective-permute-done((bf16[1,34,256]{2,1,0:T(8,128)(2,1)S(1)}, bf16[1,34,256]{2,1,0:T(8,128)(2,1)S(1)}, u32[]{:S(2)}, u32[]{:S(2)}) %collective-permute-start.15) | collective-permute-done | bytes 17440 | tf_op jit(solution)/shard_map/ppermute | solution.py:18
  113.9 2.6 collective-permute-start.17
  118.0 1.9 collective-permute-start.18
  121.5 4.1 %collective-permute-done.19 = bf16[1,34,256]{2,1,0:T(8,128)(2,1)S(1)} collective-permute-done((bf16[1,34,256]{2,1,0:T(8,128)(2,1)S(1)}, bf16[1,34,256]{2,1,0:T(8,128)(2,1)S(1)}, u32[]{:S(2)}, u32[]{:S(2)}) %collective-permute-start.19) | collective-permute-done | bytes 17440 | tf_op jit(solution)/shard_map/ppermute | solution.py:18
  129.8 2.6 collective-permute-start.21
  133.9 1.9 collective-permute-start.22
  135.8 1.5 collective-permute-start.23
  137.3 3.3 %pad_maximum_fusion = f32[3,3,3,256,256]{4,3,2,1,0:T(8,128)} fusion(f32[1,3,3,256,256]{4,3,2,1,0:T(8,128)S(1)} %maximum_multiply_fusion.2, f32[1,3,3,256,256]{4,3,2,1,0:T(8,128)S(1)} %maximum_multiply_fusion.1, f32[1,3,3,256,256]{4,3,2,1,0:T(8,128)S(1)} %maximum_multiply_fusion), kind=kLoop, calls=%fused_computation.11 | loop fusion | flops 3538944 | bytes 14155776 | tf_op jit(solution)/shard_map/stack | solution.py:139
  144.1 12.1 %gather_fusion = bf16[4096,128]{1,0:T(8,128)(2,1)S(1)} fusion(bf16[512,128]{1,0:T(8,128)(2,1)S(1)} %fusion.16, s32[4096]{0:T(1024)S(1)} %bitcast_clamp_fusion), kind=kCustom, calls=%fused_computation | custom fusion | bytes 2113536 | tf_op jit(solution)/shard_map/jit(_take)/gather | solution.py:142
  156.2 2.5 select_select_fusion
  158.7 3.7 %all-to-all-start.2 = ((bf16[32,128,128]{2,1,0:T(8,128)(2,1)}), bf16[32,128,128]{2,1,0:T(8,128)(2,1)S(1)}, u32[]{:S(2)}, u32[]{:S(2)}) async-start(bf16[32,128,128]{2,1,0:T(8,128)(2,1)} %select_select_fusion), calls=%async_computation.2 | async-start | bytes 2097152 | tf_op jit(solution)/shard_map/all_to_all | solution.py:144
  162.4 143.6 %all-reduce.2 = (bf16[3,3,3,256,256]{4,3,2,1,0:T(8,128)(2,1)}, bf16[128,256]{1,0:T(8,128)(2,1)}) all-reduce(f32[3,3,3,256,256]{4,3,2,1,0:T(8,128)} %pad_maximum_fusion, f32[128,256]{1,0:T(8,128)S(1)} %convolution_multiply_fusion.1), channel_id=1, replica_groups=mesh['lon'=8,'lat'=4] {'lon','lat'}, use_global_device_ids=true, to_apply=%region_3.4 | all-reduce | flops 1802240 | bytes 10813440 | tf_op jit(solution)/shard_map/psum | solution.py:139
  (160 shorter events, 38.6 us)
Async XLA Ops:
  0.6 47.3 %copy-start = (bf16[128,256]{1,0:T(8,128)(2,1)S(1)}, bf16[128,256]{1,0:T(8,128)(2,1)}, u32[]{:S(2)}) copy-start(bf16[128,256]{1,0:T(8,128)(2,1)} %param.12) | copy-start | bytes 196612
  15.7 27.7 %all-to-all-start.1 = ((bf16[32,128,128]{2,1,0:T(8,128)(2,1)}), bf16[32,128,128]{2,1,0:T(8,128)(2,1)S(1)}, u32[]{:S(2)}, u32[]{:S(2)}) async-start(bf16[32,128,128]{2,1,0:T(8,128)(2,1)} %bitcast.265), calls=%async_computation.1 | async-start | bytes 2097152 | tf_op jit(solution)/shard_map/all_to_all | solution.py:51
  47.9 15.8 %copy-start.2 = (bf16[3,3,3,256,256]{4,3,2,1,0:T(8,128)(2,1)S(1)}, bf16[3,3,3,256,256]{4,3,2,1,0:T(8,128)(2,1)}, u32[]{:S(2)}) copy-start(bf16[3,3,3,256,256]{4,3,2,1,0:T(8,128)(2,1)} %param.14) | copy-start | bytes 10616836
  47.9 15.8 %copy-start.3 = (pred[8,5]{0,1:T(8,128)(4,1)S(1)}, pred[8,5]{0,1:T(8,128)(4,1)}, u32[]{:S(2)}) copy-start(pred[8,5]{0,1:T(8,128)(4,1)} %constant.95) | copy-start | bytes 124
  48.2 4.1 %collective-permute-start = (bf16[16,1,256]{2,1,0:T(2,128)(2,1)S(1)}, bf16[16,1,256]{2,1,0:T(2,128)(2,1)S(1)}, u32[]{:S(2)}, u32[]{:S(2)}) collective-permute-start(bf16[16,1,256]{2,1,0:T(2,128)(2,1)S(1)} %get-tuple-element.178), channel_id=1, source_target_pairs={{0,4},{4,8},{8,12},{12,16},{16,20},{20,24},{24,28},{28,0},{1,5},{5... | collective-permute-start | bytes 24584 | tf_op jit(solution)/shard_map/ppermute | solution.py:15
  49.9 2.6 collective-permute-start.1
  52.4 6.6 %collective-permute-start.2 = (bf16[1,34,256]{2,1,0:T(8,128)(2,1)S(1)}, bf16[1,34,256]{2,1,0:T(8,128)(2,1)S(1)}, u32[]{:S(2)}, u32[]{:S(2)}) collective-permute-start(bf16[1,34,256]{2,1,0:T(8,128)(2,1)S(1)} %get-tuple-element.166), channel_id=1, source_target_pairs={{0,1},{1,2},{2,3},{4,5},{5,6},{6,7},{8,9},{9,10},{10,11},{12,13},{... | collective-permute-start | bytes 52232 | tf_op jit(solution)/shard_map/ppermute | solution.py:15
  57.5 5.7 %collective-permute-start.3 = (bf16[1,34,256]{2,1,0:T(8,128)(2,1)S(1)}, bf16[1,34,256]{2,1,0:T(8,128)(2,1)S(1)}, u32[]{:S(2)}, u32[]{:S(2)}) collective-permute-start(bf16[1,34,256]{2,1,0:T(8,128)(2,1)S(1)} %get-tuple-element.167), channel_id=1, source_target_pairs={{1,0},{2,1},{3,2},{5,4},{6,5},{7,6},{9,8},{10,9},{11,10},{13,12},{... | collective-permute-start | bytes 52232 | tf_op jit(solution)/shard_map/ppermute | solution.py:18
  65.3 4.1 %collective-permute-start.4 = (bf16[16,1,256]{2,1,0:T(2,128)(2,1)S(1)}, bf16[16,1,256]{2,1,0:T(2,128)(2,1)S(1)}, u32[]{:S(2)}, u32[]{:S(2)}) collective-permute-start(bf16[16,1,256]{2,1,0:T(2,128)(2,1)S(1)} %get-tuple-element.176), channel_id=1, source_target_pairs={{0,4},{4,8},{8,12},{12,16},{16,20},{20,24},{24,28},{28,0},{1,5},{5... | collective-permute-start | bytes 24584 | tf_op jit(solution)/shard_map/ppermute | solution.py:15
  65.4 4.1 %collective-permute-start.5 = (bf16[16,1,256]{2,1,0:T(2,128)(2,1)S(1)}, bf16[16,1,256]{2,1,0:T(2,128)(2,1)S(1)}, u32[]{:S(2)}, u32[]{:S(2)}) collective-permute-start(bf16[16,1,256]{2,1,0:T(2,128)(2,1)S(1)} %get-tuple-element.177), channel_id=1, source_target_pairs={{4,0},{8,4},{12,8},{16,12},{20,16},{24,20},{28,24},{0,28},{5,1},{9... | collective-permute-start | bytes 24584 | tf_op jit(solution)/shard_map/ppermute | solution.py:18
  69.5 3.4 %collective-permute-start.6 = (bf16[1,34,256]{2,1,0:T(8,128)(2,1)S(1)}, bf16[1,34,256]{2,1,0:T(8,128)(2,1)S(1)}, u32[]{:S(2)}, u32[]{:S(2)}) collective-permute-start(bf16[1,34,256]{2,1,0:T(8,128)(2,1)S(1)} %get-tuple-element.164), channel_id=1, source_target_pairs={{0,1},{1,2},{2,3},{4,5},{5,6},{6,7},{8,9},{9,10},{10,11},{12,13},{... | collective-permute-start | bytes 52232 | tf_op jit(solution)/shard_map/ppermute | solution.py:15
  71.4 5.7 %collective-permute-start.7 = (bf16[1,34,256]{2,1,0:T(8,128)(2,1)S(1)}, bf16[1,34,256]{2,1,0:T(8,128)(2,1)S(1)}, u32[]{:S(2)}, u32[]{:S(2)}) collective-permute-start(bf16[1,34,256]{2,1,0:T(8,128)(2,1)S(1)} %get-tuple-element.165), channel_id=1, source_target_pairs={{1,0},{2,1},{3,2},{5,4},{6,5},{7,6},{9,8},{10,9},{11,10},{13,12},{... | collective-permute-start | bytes 52232 | tf_op jit(solution)/shard_map/ppermute | solution.py:18
  79.1 4.1 %collective-permute-start.8 = (bf16[16,1,256]{2,1,0:T(2,128)(2,1)S(1)}, bf16[16,1,256]{2,1,0:T(2,128)(2,1)S(1)}, u32[]{:S(2)}, u32[]{:S(2)}) collective-permute-start(bf16[16,1,256]{2,1,0:T(2,128)(2,1)S(1)} %get-tuple-element.174), channel_id=1, source_target_pairs={{0,4},{4,8},{8,12},{12,16},{16,20},{20,24},{24,28},{28,0},{1,5},{5... | collective-permute-start | bytes 24584 | tf_op jit(solution)/shard_map/ppermute | solution.py:15
  79.2 4.1 %collective-permute-start.9 = (bf16[16,1,256]{2,1,0:T(2,128)(2,1)S(1)}, bf16[16,1,256]{2,1,0:T(2,128)(2,1)S(1)}, u32[]{:S(2)}, u32[]{:S(2)}) collective-permute-start(bf16[16,1,256]{2,1,0:T(2,128)(2,1)S(1)} %get-tuple-element.175), channel_id=1, source_target_pairs={{4,0},{8,4},{12,8},{16,12},{20,16},{24,20},{28,24},{0,28},{5,1},{9... | collective-permute-start | bytes 24584 | tf_op jit(solution)/shard_map/ppermute | solution.py:18
  83.3 4.5 %collective-permute-start.10 = (bf16[1,34,256]{2,1,0:T(8,128)(2,1)S(1)}, bf16[1,34,256]{2,1,0:T(8,128)(2,1)S(1)}, u32[]{:S(2)}, u32[]{:S(2)}) collective-permute-start(bf16[1,34,256]{2,1,0:T(8,128)(2,1)S(1)} %get-tuple-element.162), channel_id=1, source_target_pairs={{0,1},{1,2},{2,3},{4,5},{5,6},{6,7},{8,9},{9,10},{10,11},{12,13},{... | collective-permute-start | bytes 52232 | tf_op jit(solution)/shard_map/ppermute | solution.py:15
  86.3 5.7 %collective-permute-start.11 = (bf16[1,34,256]{2,1,0:T(8,128)(2,1)S(1)}, bf16[1,34,256]{2,1,0:T(8,128)(2,1)S(1)}, u32[]{:S(2)}, u32[]{:S(2)}) collective-permute-start(bf16[1,34,256]{2,1,0:T(8,128)(2,1)S(1)} %get-tuple-element.163), channel_id=1, source_target_pairs={{1,0},{2,1},{3,2},{5,4},{6,5},{7,6},{9,8},{10,9},{11,10},{13,12},{... | collective-permute-start | bytes 52232 | tf_op jit(solution)/shard_map/ppermute | solution.py:18
  93.4 1.0 copy-start.1
  97.6 4.1 %collective-permute-start.12 = (bf16[16,1,256]{2,1,0:T(2,128)(2,1)S(1)}, bf16[16,1,256]{2,1,0:T(2,128)(2,1)S(1)}, u32[]{:S(2)}, u32[]{:S(2)}) collective-permute-start(bf16[16,1,256]{2,1,0:T(2,128)(2,1)S(1)} %get-tuple-element.172), channel_id=1, source_target_pairs={{0,4},{4,8},{8,12},{12,16},{16,20},{20,24},{24,28},{28,0},{1,5},{5... | collective-permute-start | bytes 24584 | tf_op jit(solution)/shard_map/ppermute | solution.py:15
  97.7 4.1 %collective-permute-start.13 = (bf16[16,1,256]{2,1,0:T(2,128)(2,1)S(1)}, bf16[16,1,256]{2,1,0:T(2,128)(2,1)S(1)}, u32[]{:S(2)}, u32[]{:S(2)}) collective-permute-start(bf16[16,1,256]{2,1,0:T(2,128)(2,1)S(1)} %get-tuple-element.173), channel_id=1, source_target_pairs={{4,0},{8,4},{12,8},{16,12},{20,16},{24,20},{28,24},{0,28},{5,1},{9... | collective-permute-start | bytes 24584 | tf_op jit(solution)/shard_map/ppermute | solution.py:18
  101.8 3.5 %collective-permute-start.14 = (bf16[1,34,256]{2,1,0:T(8,128)(2,1)S(1)}, bf16[1,34,256]{2,1,0:T(8,128)(2,1)S(1)}, u32[]{:S(2)}, u32[]{:S(2)}) collective-permute-start(bf16[1,34,256]{2,1,0:T(8,128)(2,1)S(1)} %get-tuple-element.158), channel_id=1, source_target_pairs={{0,1},{1,2},{2,3},{4,5},{5,6},{6,7},{8,9},{9,10},{10,11},{12,13},{... | collective-permute-start | bytes 52232 | tf_op jit(solution)/shard_map/ppermute | solution.py:15
  103.7 5.7 %collective-permute-start.15 = (bf16[1,34,256]{2,1,0:T(8,128)(2,1)S(1)}, bf16[1,34,256]{2,1,0:T(8,128)(2,1)S(1)}, u32[]{:S(2)}, u32[]{:S(2)}) collective-permute-start(bf16[1,34,256]{2,1,0:T(8,128)(2,1)S(1)} %get-tuple-element.159), channel_id=1, source_target_pairs={{1,0},{2,1},{3,2},{5,4},{6,5},{7,6},{9,8},{10,9},{11,10},{13,12},{... | collective-permute-start | bytes 52232 | tf_op jit(solution)/shard_map/ppermute | solution.py:18
  113.8 4.1 %collective-permute-start.16 = (bf16[16,1,256]{2,1,0:T(2,128)(2,1)S(1)}, bf16[16,1,256]{2,1,0:T(2,128)(2,1)S(1)}, u32[]{:S(2)}, u32[]{:S(2)}) collective-permute-start(bf16[16,1,256]{2,1,0:T(2,128)(2,1)S(1)} %get-tuple-element.170), channel_id=1, source_target_pairs={{0,4},{4,8},{8,12},{12,16},{16,20},{20,24},{24,28},{28,0},{1,5},{5... | collective-permute-start | bytes 24584 | tf_op jit(solution)/shard_map/ppermute | solution.py:15
  113.9 4.1 %collective-permute-start.17 = (bf16[16,1,256]{2,1,0:T(2,128)(2,1)S(1)}, bf16[16,1,256]{2,1,0:T(2,128)(2,1)S(1)}, u32[]{:S(2)}, u32[]{:S(2)}) collective-permute-start(bf16[16,1,256]{2,1,0:T(2,128)(2,1)S(1)} %get-tuple-element.171), channel_id=1, source_target_pairs={{4,0},{8,4},{12,8},{16,12},{20,16},{24,20},{28,24},{0,28},{5,1},{9... | collective-permute-start | bytes 24584 | tf_op jit(solution)/shard_map/ppermute | solution.py:18
  118.0 3.5 %collective-permute-start.18 = (bf16[1,34,256]{2,1,0:T(8,128)(2,1)S(1)}, bf16[1,34,256]{2,1,0:T(8,128)(2,1)S(1)}, u32[]{:S(2)}, u32[]{:S(2)}) collective-permute-start(bf16[1,34,256]{2,1,0:T(8,128)(2,1)S(1)} %get-tuple-element.154), channel_id=1, source_target_pairs={{0,1},{1,2},{2,3},{4,5},{5,6},{6,7},{8,9},{9,10},{10,11},{12,13},{... | collective-permute-start | bytes 52232 | tf_op jit(solution)/shard_map/ppermute | solution.py:15
  119.9 5.7 %collective-permute-start.19 = (bf16[1,34,256]{2,1,0:T(8,128)(2,1)S(1)}, bf16[1,34,256]{2,1,0:T(8,128)(2,1)S(1)}, u32[]{:S(2)}, u32[]{:S(2)}) collective-permute-start(bf16[1,34,256]{2,1,0:T(8,128)(2,1)S(1)} %get-tuple-element.155), channel_id=1, source_target_pairs={{1,0},{2,1},{3,2},{5,4},{6,5},{7,6},{9,8},{10,9},{11,10},{13,12},{... | collective-permute-start | bytes 52232 | tf_op jit(solution)/shard_map/ppermute | solution.py:18
  129.7 4.1 %collective-permute-start.20 = (bf16[16,1,256]{2,1,0:T(2,128)(2,1)S(1)}, bf16[16,1,256]{2,1,0:T(2,128)(2,1)S(1)}, u32[]{:S(2)}, u32[]{:S(2)}) collective-permute-start(bf16[16,1,256]{2,1,0:T(2,128)(2,1)S(1)} %get-tuple-element.168), channel_id=1, source_target_pairs={{0,4},{4,8},{8,12},{12,16},{16,20},{20,24},{24,28},{28,0},{1,5},{5... | collective-permute-start | bytes 24584 | tf_op jit(solution)/shard_map/ppermute | solution.py:15
  129.8 4.1 %collective-permute-start.21 = (bf16[16,1,256]{2,1,0:T(2,128)(2,1)S(1)}, bf16[16,1,256]{2,1,0:T(2,128)(2,1)S(1)}, u32[]{:S(2)}, u32[]{:S(2)}) collective-permute-start(bf16[16,1,256]{2,1,0:T(2,128)(2,1)S(1)} %get-tuple-element.169), channel_id=1, source_target_pairs={{4,0},{8,4},{12,8},{16,12},{20,16},{24,20},{28,24},{0,28},{5,1},{9... | collective-permute-start | bytes 24584 | tf_op jit(solution)/shard_map/ppermute | solution.py:18
  133.9 6.8 %collective-permute-start.22 = (bf16[1,34,256]{2,1,0:T(8,128)(2,1)S(1)}, bf16[1,34,256]{2,1,0:T(8,128)(2,1)S(1)}, u32[]{:S(2)}, u32[]{:S(2)}) collective-permute-start(bf16[1,34,256]{2,1,0:T(8,128)(2,1)S(1)} %get-tuple-element.150), channel_id=1, source_target_pairs={{0,1},{1,2},{2,3},{4,5},{5,6},{6,7},{8,9},{9,10},{10,11},{12,13},{... | collective-permute-start | bytes 52232 | tf_op jit(solution)/shard_map/ppermute | solution.py:15
  135.8 5.7 %collective-permute-start.23 = (bf16[1,34,256]{2,1,0:T(8,128)(2,1)S(1)}, bf16[1,34,256]{2,1,0:T(8,128)(2,1)S(1)}, u32[]{:S(2)}, u32[]{:S(2)}) collective-permute-start(bf16[1,34,256]{2,1,0:T(8,128)(2,1)S(1)} %get-tuple-element.151), channel_id=1, source_target_pairs={{1,0},{2,1},{3,2},{5,4},{6,5},{7,6},{9,8},{10,9},{11,10},{13,12},{... | collective-permute-start | bytes 52232 | tf_op jit(solution)/shard_map/ppermute | solution.py:18
  158.7 147.3 %all-to-all-start.2 = ((bf16[32,128,128]{2,1,0:T(8,128)(2,1)}), bf16[32,128,128]{2,1,0:T(8,128)(2,1)S(1)}, u32[]{:S(2)}, u32[]{:S(2)}) async-start(bf16[32,128,128]{2,1,0:T(8,128)(2,1)} %select_select_fusion), calls=%async_computation.2 | async-start | bytes 2097152 | tf_op jit(solution)/shard_map/all_to_all | solution.py:144
where the time goes:
time: 308 us; the launch traced here: 307 us
  blocking collectives  158 us (51%)
  waiting for transfers between devices  52 us (17%)
  starting transfers between devices  46.3 us (15%)
  matrix products  17.1 us (6%)
  local copies, waits for them, and re-layouts  16.8 us (5%)
  other arithmetic  15.2 us (5%)
    psum x1, blocking collectives, on_device(): lax.psum((jnp.stack(kernel_grads), embed_grad), ('lon', 'lat'))  144 us
    all_to_all x1, waiting for transfers between devices, on_device(): lax.all_to_all(obs_rows, ('lon', 'lat'), split_axis=0, concat_axis=0, til...  24.4 us
    ppermute x12, starting transfers between devices, extended(): lax.ppermute(lax.slice_in_dim(block, 0, width, axis=dim), axis, backward)  22.2 us
    ppermute x12, waiting for transfers between devices, extended(): lax.ppermute(lax.slice_in_dim(block, 0, width, axis=dim), axis, backward)  21.9 us
    ppermute x12, starting transfers between devices, extended(): lax.ppermute(lax.slice_in_dim(block, block.shape[dim] - width, None, axis...  17.7 us
    all_to_all x1, blocking collectives, on_device(): lax.all_to_all(sent_ids, ('lon', 'lat'), split_axis=0, concat_axis=0, til...  14.3 us
    gather x1, local copies, waits for them, and re-layouts, on_device(): picked = jnp.take(cell_grad, jnp.maximum(got_ids, 0), axis=0)  12.1 us
    dot_general x27, matrix products, on_device(): lax.dot_general(window, slope_flat, (((0,), (0,)), ((), ())), preferred_e...  7.3 us
  transfers between devices with their start and end apart: 26, of which 16 were waited for; matrix products, arithmetic and copies ran while one was open for 2% of the time, Pallas kernels for 0%

commit v1 on v0

--- a/solution.py
+++ b/solution.py
@@ -136,7 +136,9 @@
         )
         * inv_root[:, None]
     ).astype(jnp.bfloat16)
-    kernel_total, embed_total = lax.psum((jnp.stack(kernel_grads), embed_grad), ("lon", "lat"))
+    kernel_total, embed_total = lax.psum(
+        lax.psum((jnp.stack(kernel_grads), embed_grad), "lat"), "lon"
+    )
     kernel_out = kernel_total.astype(jnp.bfloat16)
     embed_out = embed_total.astype(jnp.bfloat16)
     picked = jnp.take(cell_grad, jnp.maximum(got_ids, 0), axis=0)

time: 308 us -> 580 us (1.88)
  waiting for transfers between devices: 52 us -> 256 us
  blocking collectives: 158 us -> 217 us
  between operations: 1.63 us -> 15 us
    psum x0 -> x1, waiting for transfers between devices: none -> 204 us  [on_device(): lax.psum((jnp.stack(kernel_grads), embed_grad), 'lat')]
    all_to_all x0 -> x1, blocking collectives: none -> 56.4 us  [on_device(): lax.all_to_all(picked, ('lon', 'lat'), split_axis=0, concat_axis=0, tiled...]
  transfers between devices with their start and end apart: 26 -> 26, of which waited for: 16 -> 17; matrix products, arithmetic and copies ran while one was open for 2% -> 4% of each run, Pallas kernels for 0% -> 0%
where the time goes in v1:
time: 580 us; the launch traced here: 579 us
  waiting for transfers between devices  256 us (44%)
  blocking collectives  217 us (37%)
  starting transfers between devices  42.6 us (7%)
  matrix products  17.7 us (3%)
  local copies, waits for them, and re-layouts  16.8 us (3%)
  between operations  15 us (3%)
  other arithmetic  14.3 us (2%)
    psum x1, waiting for transfers between devices, on_device(): lax.psum((jnp.stack(kernel_grads), embed_grad), 'lat')  204 us
    psum x1, blocking collectives, on_device(): lax.psum(lax.psum((jnp.stack(kernel_grads), embed_grad), 'lat'), 'lon')  146 us
    all_to_all x1, blocking collectives, on_device(): lax.all_to_all(picked, ('lon', 'lat'), split_axis=0, concat_axis=0, tiled...  56.4 us
    all_to_all x1, waiting for transfers between devices, on_device(): lax.all_to_all(obs_rows, ('lon', 'lat'), split_axis=0, concat_axis=0, til...  24.3 us
    ppermute x12, starting transfers between devices, extended(): lax.ppermute(lax.slice_in_dim(block, 0, width, axis=dim), axis, backward)  22.2 us
    ppermute x12, waiting for transfers between devices, extended(): lax.ppermute(lax.slice_in_dim(block, 0, width, axis=dim), axis, backward)  21.8 us
    ppermute x12, starting transfers between devices, extended(): lax.ppermute(lax.slice_in_dim(block, block.shape[dim] - width, None, axis...  17.7 us
    all_to_all x1, blocking collectives, on_device(): lax.all_to_all(sent_ids, ('lon', 'lat'), split_axis=0, concat_axis=0, til...  14.3 us
  transfers between devices with their start and end apart: 26, of which 17 were waited for; matrix products, arithmetic and copies ran while one was open for 4% of the time, Pallas kernels for 0%

profile of v1, /device:TPU:0, one launch (start us, length us, event | category | flops | bytes accessed | tf_op | source)
XLA Modules:
  0.0 579.2 jit_solution(8625960131877601455)
XLA Ops:
  8.0 14.3 %all_to_all.33 = s32[32,128,1]{1,2,0:T(1,128)S(1)} all-to-all(s32[32,128,1]{1,2,0:T(1,128)S(1)} %bitcast.270), channel_id=1, replica_groups=mesh['lon'=8,'lat'=4] {'lon','lat'}, dimensions={0} | all-to-all | bytes 32768 | tf_op jit(solution)/shard_map/all_to_all | solution.py:52
  22.3 2.6 all-to-all-start.1
  25.7 24.3 %all-to-all-done.1 = bf16[32,128,128]{2,1,0:T(8,128)(2,1)S(1)} async-done(((bf16[32,128,128]{2,1,0:T(8,128)(2,1)}), bf16[32,128,128]{2,1,0:T(8,128)(2,1)S(1)}, u32[]{:S(2)}, u32[]{:S(2)}) %all-to-all-start.1) | async-done | bytes 1048608 | tf_op jit(solution)/shard_map/all_to_all | solution.py:51
  50.0 4.4 while.16
  50.5 1.6 fusion.171
  52.8 1.6 fusion.171
  54.8 1.6 collective-permute-start
  57.5 1.4 collective-permute-done
  59.0 5.1 collective-permute-start.2
  65.5 4.2 collective-permute-done.3
  71.9 2.6 collective-permute-start.5
  74.5 1.4 collective-permute-done.4
  76.0 1.9 collective-permute-start.6
  79.4 4.2 collective-permute-done.7
  85.7 2.6 collective-permute-start.9
  89.8 3.0 collective-permute-start.10
  94.4 4.1 collective-permute-done.11
  104.2 2.6 collective-permute-start.13
  108.3 1.9 collective-permute-start.14
  111.8 4.1 collective-permute-done.15
  120.4 2.6 collective-permute-start.17
  124.5 1.9 collective-permute-start.18
  128.0 4.1 collective-permute-done.19
  136.3 2.6 collective-permute-start.21
  140.4 1.9 collective-permute-start.22
  142.3 1.5 collective-permute-start.23
  143.9 3.4 pad_maximum_fusion
  151.3 12.1 %gather_fusion = bf16[4096,128]{1,0:T(8,128)(2,1)S(1)} fusion(bf16[512,128]{1,0:T(8,128)(2,1)S(1)} %fusion.16, s32[4096]{0:T(1024)S(1)} %bitcast_clamp_fusion), kind=kCustom, calls=%fused_computation | custom fusion | bytes 2113536 | tf_op jit(solution)/shard_map/jit(_take)/gather | solution.py:144
  163.4 1.4 select_select_fusion
  164.8 56.4 %all_to_all.34 = bf16[32,128,128]{2,1,0:T(8,128)(2,1)S(1)} all-to-all(bf16[32,128,128]{2,1,0:T(8,128)(2,1)S(1)} %select_select_fusion), channel_id=1, replica_groups=mesh['lon'=8,'lat'=4] {'lon','lat'}, dimensions={0} | all-to-all | bytes 2097152 | tf_op jit(solution)/shard_map/all_to_all | solution.py:146
  221.2 204.3 %all-reduce.5.cloned.1.call-done = (f32[3,3,3,256,256]{4,3,2,1,0:T(8,128)}, f32[128,256]{1,0:T(8,128)}) async-done(((f32[3,3,3,256,256]{4,3,2,1,0:T(8,128)}, f32[128,256]{1,0:T(8,128)}), (f32[3,3,3,256,256]{4,3,2,1,0:T(8,128)}, f32[128,256]{1,0:T(8,128)})) %all-reduce.5.cloned.1.call-update) | async-done | bytes 7208976 | tf_op jit(solution)/shard_map/psum | solution.py:140
  425.5 145.9 %all-reduce.6 = (bf16[3,3,3,256,256]{4,3,2,1,0:T(8,128)(2,1)}, bf16[128,256]{1,0:T(8,128)(2,1)}) all-reduce(f32[3,3,3,256,256]{4,3,2,1,0:T(8,128)} %get-tuple-element.148, f32[128,256]{1,0:T(8,128)} %get-tuple-element.149), channel_id=1, replica_groups=mesh['lon'=8,'lat'=4] {'lon'}, use_global_device_ids=true, to_apply=%region_4.5 | all-reduce | flops 1802240 | bytes 10813440 | tf_op jit(solution)/shard_map/psum | solution.py:139
  (162 shorter events, 40.5 us)
Async XLA Ops:
  7.2 47.3 %copy-start = (bf16[128,256]{1,0:T(8,128)(2,1)S(1)}, bf16[128,256]{1,0:T(8,128)(2,1)}, u32[]{:S(2)}) copy-start(bf16[128,256]{1,0:T(8,128)(2,1)} %param.12) | copy-start | bytes 196612
  22.3 27.7 %all-to-all-start.1 = ((bf16[32,128,128]{2,1,0:T(8,128)(2,1)}), bf16[32,128,128]{2,1,0:T(8,128)(2,1)S(1)}, u32[]{:S(2)}, u32[]{:S(2)}) async-start(bf16[32,128,128]{2,1,0:T(8,128)(2,1)} %bitcast.265), calls=%async_computation.1 | async-start | bytes 2097152 | tf_op jit(solution)/shard_map/all_to_all | solution.py:51
  24.9 400.5 %all-reduce.5.cloned.1.call-start = ((), (), s32[]{:S(2)}) async-start(), calls=%async_computation.3 | async-start | bytes 14417920 | tf_op jit(solution)/shard_map/psum | solution.py:140
  54.4 15.8 %copy-start.2 = (bf16[3,3,3,256,256]{4,3,2,1,0:T(8,128)(2,1)S(1)}, bf16[3,3,3,256,256]{4,3,2,1,0:T(8,128)(2,1)}, u32[]{:S(2)}) copy-start(bf16[3,3,3,256,256]{4,3,2,1,0:T(8,128)(2,1)} %param.14) | copy-start | bytes 10616836
  54.4 15.8 %copy-start.3 = (pred[8,5]{0,1:T(8,128)(4,1)S(1)}, pred[8,5]{0,1:T(8,128)(4,1)}, u32[]{:S(2)}) copy-start(pred[8,5]{0,1:T(8,128)(4,1)} %constant.95) | copy-start | bytes 124
  54.8 4.1 collective-permute-start
  56.4 2.6 collective-permute-start.1
  59.0 6.6 %collective-permute-start.2 = (bf16[1,34,256]{2,1,0:T(8,128)(2,1)S(1)}, bf16[1,34,256]{2,1,0:T(8,128)(2,1)S(1)}, u32[]{:S(2)}, u32[]{:S(2)}) collective-permute-start(bf16[1,34,256]{2,1,0:T(8,128)(2,1)S(1)} %get-tuple-element.168), channel_id=1, source_target_pairs={{0,1},{1,2},{2,3},{4,5},{5,6},{6,7},{8,9},{9,10},{10,11},{12,13},{... | collective-permute-start | bytes 52232 | tf_op jit(solution)/shard_map/ppermute | solution.py:15
  64.1 5.7 collective-permute-start.3
  71.8 4.1 collective-permute-start.4
  71.9 4.1 collective-permute-start.5
  76.0 3.4 collective-permute-start.6
  77.9 5.7 collective-permute-start.7
  85.7 4.1 collective-permute-start.8
  85.7 4.1 collective-permute-start.9
  89.8 4.5 collective-permute-start.10
  92.8 5.7 collective-permute-start.11
  99.9 1.0 copy-start.1
  104.2 4.1 collective-permute-start.12
  104.2 4.1 collective-permute-start.13
  108.3 3.5 collective-permute-start.14
  110.3 5.7 collective-permute-start.15
  120.3 4.1 collective-permute-start.16
  120.4 4.1 collective-permute-start.17
  124.5 3.5 collective-permute-start.18
  126.4 5.7 collective-permute-start.19
  136.3 4.1 collective-permute-start.20
  136.3 4.1 collective-permute-start.21
  140.4 6.8 %collective-permute-start.22 = (bf16[1,34,256]{2,1,0:T(8,128)(2,1)S(1)}, bf16[1,34,256]{2,1,0:T(8,128)(2,1)S(1)}, u32[]{:S(2)}, u32[]{:S(2)}) collective-permute-start(bf16[1,34,256]{2,1,0:T(8,128)(2,1)S(1)} %get-tuple-element.152), channel_id=1, source_target_pairs={{0,1},{1,2},{2,3},{4,5},{5,6},{6,7},{8,9},{9,10},{10,11},{12,13},{... | collective-permute-start | bytes 52232 | tf_op jit(solution)/shard_map/ppermute | solution.py:15
  142.3 5.7 collective-permute-start.23
Sparse Core Ops, SparseCore 0:
  151.1 274.2 all-reduce.4
